TPU v7x, 32 devices: a whole 2x2x4 slice. The times are simulated.
32 devices in a mesh: parts: 2 (over y), fsdp: 4 (over z), seq: 2 (over x), ctx: 2 (over core).
Axes of the slice: x: 2, y: 2, z: 4, core: 2. Of those that a mesh axis runs over, the one named last changes fastest.
Arguments:
- hidden_in: bfloat16 [8, 2, 96, 8192], P(('parts', 'fsdp'), 'ctx', None, 'seq'), parts along dimension 0, may hold values from -6 to 6
- weight: bfloat16 [8192, 4096], P('fsdp', 'seq'), may hold values from -0.0625 to 0.0625
- clip_upper: float32 [128, 4096], P(('parts', 'fsdp'), 'seq'), parts along dimension 0, may hold values from 0.5 to 3
- clip_lower: float32 [128, 4096], P(('parts', 'fsdp'), 'seq'), parts along dimension 0, may hold values from -0.5 to 2.5
- filters: float32 [256, 7], P('seq'), may hold values from -3 to 3
- gate: bfloat16 [8, 2, 96, 4096], P(('parts', 'fsdp'), 'ctx', None, 'seq'), parts along dimension 0, may hold values from -6 to 6
- target: bfloat16 [8, 2, 96, 4096], P(('parts', 'fsdp'), 'ctx', None, 'seq'), parts along dimension 0, may hold values from -6 to 6
Outputs:
- grad_upper: float32 [128, 4096], P(('parts', 'fsdp'), 'seq'), parts along dimension 0
- grad_lower: float32 [128, 4096], P(('parts', 'fsdp'), 'seq'), parts along dimension 0
There are 2 independent parts, one for each index of `parts`. A program takes and returns all parts, laid end to end along the dimension named above; an argument that names none is the same for every part. Nothing has to cross between parts.
All inputs are finite; a program needn't handle non-finite values.
Results may differ from a plain program's by a relative error of at most 0.0039.
Values may be sent and summed in bfloat16 or wider, within the bound.
No kernel may reach another device: no remote copies, remote signals or barrier semaphores. Data moves between devices by JAX's collectives and lax.ppermute only.
A program may use at most 128 MiB of HBM per device.

v0:
```python
import jax
import jax.numpy as jnp
from jax import lax
from jax.sharding import PartitionSpec as P

FILT = 7
CGROUP = 16


def from_behind(value, axis, by):
    devices = lax.axis_size(axis)
    pairs = [(i, i + by) for i in range(devices) if 0 <= i + by < devices]
    return lax.ppermute(value, axis, pairs)


def soft_clip(values, upper_logit, lower_logit):
    rows = values.shape[0]
    groups = upper_logit.shape[0]
    blocks = values.reshape(groups, rows // groups, values.shape[1])
    amax = jnp.max(jnp.abs(blocks), axis=1) + 1e-06
    upper = jax.nn.sigmoid(upper_logit) * amax
    lower = -jax.nn.sigmoid(lower_logit) * amax
    center = ((upper + lower) * 0.5)[:, None, :]
    radius = ((upper - lower) * 0.5)[:, None, :]
    clipped = center + radius * jnp.tanh((blocks - center) / radius)
    return clipped.reshape(rows, values.shape[1])


def on_device(hidden_in, weight, clip_upper, clip_lower, filters, gate, target):
    shards = lax.axis_size("fsdp")
    width = hidden_in.shape[-1]
    local_rows = hidden_in.reshape(-1, width)
    length = local_rows.shape[0]
    rows, columns = weight.shape
    features = lax.all_gather(local_rows, "seq", axis=1, tiled=True)
    pieces = features.reshape(length, shards, rows).transpose(1, 0, 2)
    mine = lax.all_to_all(pieces, "fsdp", 0, 0)
    inputs = mine.reshape(shards * length, rows)
    values = weight.astype(jnp.float32)
    quant = soft_clip(values, clip_upper, clip_lower).astype(jnp.bfloat16)
    partial = jnp.dot(inputs, quant, preferred_element_type=jnp.float32)
    proj = lax.psum_scatter(partial, "fsdp", scatter_dimension=0, tiled=True).astype(jnp.bfloat16)
    taps = jnp.repeat(filters, CGROUP, axis=0).T
    pad = FILT - 1
    previous = from_behind(proj[length - pad :], "ctx", 1)
    padded = jnp.concatenate([previous, proj], axis=0).astype(jnp.float32)
    conv = jnp.zeros((length, columns), jnp.float32)
    for tap in range(FILT):
        conv = conv + taps[tap] * padded[pad - tap : pad - tap + length]
    gates = gate.reshape(length, columns).astype(jnp.float32)
    wanted = target.reshape(length, columns).astype(jnp.float32)
    total_tokens = lax.axis_size("fsdp") * lax.axis_size("ctx") * length
    scale = 1024.0 / jnp.sqrt(jnp.float32(total_tokens))
    d_conv = scale * (gates * conv - wanted) * gates
    following = from_behind(d_conv[:pad], "ctx", -1)
    padded_back = jnp.concatenate([d_conv, following], axis=0)
    d_proj = jnp.zeros((length, columns), jnp.float32)
    for tap in range(FILT):
        d_proj = d_proj + taps[tap] * padded_back[tap : tap + length]
    d_proj = d_proj.astype(jnp.bfloat16)
    d_all = lax.all_gather(d_proj, "fsdp", axis=0, tiled=True)
    d_clipped = lax.dot_general(
        inputs, d_all, (((0,), (0,)), ((), ())), preferred_element_type=jnp.float32
    )
    _, pull = jax.vjp(
        lambda upper_logit, lower_logit: soft_clip(values, upper_logit, lower_logit),
        clip_upper,
        clip_lower,
    )
    grad_up, grad_low = pull(d_clipped)
    grad_upper, grad_lower = lax.psum((grad_up, grad_low), "ctx")
    return (grad_upper, grad_lower)


def solution(mesh):
    return jax.shard_map(
        on_device,
        mesh=mesh,
        in_specs=(
            P(("parts", "fsdp"), "ctx", None, "seq"),
            P("fsdp", "seq"),
            P(("parts", "fsdp"), "seq"),
            P(("parts", "fsdp"), "seq"),
            P("seq", None),
            P(("parts", "fsdp"), "ctx", None, "seq"),
            P(("parts", "fsdp"), "ctx", None, "seq"),
        ),
        out_specs=(P(("parts", "fsdp"), "seq"), P(("parts", "fsdp"), "seq")),
        check_vma=False,
    )
```

profile of v0, /device:TPU:0, one launch (start us, length us, event | category | flops | bytes accessed | tf_op | source)
XLA Modules:
  0.0 267.6 jit_solution(9266589008034086142)
XLA Ops:
  7.2 0.0 all-gather.6.cloned.1.call-start
  7.2 0.7 all-gather.6.cloned.1.call-update
  7.9 0.0 copy-start
  7.9 0.0 copy-start.2
  7.9 31.6 %all-gather.6.cloned.1.call-done = bf16[1,1,96,8192]{3,2,1,0:T(8,128)(2,1)} async-done(((bf16[1,1,96,4096]{3,2,1,0:T(8,128)(2,1)}), bf16[1,1,96,8192]{3,2,1,0:T(8,128)(2,1)}) %all-gather.6.cloned.1.call-update) | async-done | bytes 1572880 | tf_op jit(solution)/shard_map/all_gather | solution.py:35
  39.5 2.9 %reshape.56 = bf16[96,4,2048]{2,1,0:T(4,128)(2,1)S(1)} reshape(bf16[1,1,96,8192]{3,2,1,0:T(8,128)(2,1)} %all-gather.6.cloned.1.call-done) | data formatting | bytes 3145728 | tf_op jit(solution)/shard_map/reshape | solution.py:36
  42.4 2.1 copy.18
  44.4 4.6 %all-to-all-start = ((bf16[4,96,2048]{2,1,0:T(8,128)(2,1)}), bf16[4,96,2048]{2,1,0:T(8,128)(2,1)S(1)}, u32[]{:S(2)}, u32[]{:S(2)}) async-start(bf16[4,96,2048]{2,1,0:T(8,128)(2,1)} %copy.18), calls=%async_computation | async-start | bytes 3145728 | tf_op jit(solution)/shard_map/all_to_all | solution.py:37
  49.0 0.0 reduce-scatter.4.cloned.1.call-start
  49.0 5.7 %abs_reduce_fusion = f32[16,2048]{1,0:T(8,128)S(1)} fusion(bf16[2048,2048]{1,0:T(8,128)(2,1)} %param.8), kind=kLoop, calls=%fused_computation.11 | loop fusion | flops 12550144 | bytes 8519680 | tf_op jit(solution)/shard_map/reduce_max | solution.py:20
  54.7 0.0 copy-done
  54.8 0.8 multiply_divide_fusion
  55.5 8.8 %fusion = bf16[2048,2048]{1,0:T(8,128)(2,1)} fusion(bf16[2048,2048]{1,0:T(8,128)(2,1)} %param.8, f32[16,2048]{1,0:T(8,128)S(1)} %get-tuple-element.9, f32[16,2048]{1,0:T(8,128)S(1)} %get-tuple-element.12), kind=kLoop, calls=%fused_computation.4 | loop fusion | flops 25165824 | bytes 17039360 | tf_op jit(solution)/shard_map/convert_element_type | solution.py:40
  64.3 21.7 %all-to-all-done = bf16[4,96,2048]{2,1,0:T(8,128)(2,1)S(1)} async-done(((bf16[4,96,2048]{2,1,0:T(8,128)(2,1)}), bf16[4,96,2048]{2,1,0:T(8,128)(2,1)S(1)}, u32[]{:S(2)}, u32[]{:S(2)}) %all-to-all-start) | async-done | bytes 1572896 | tf_op jit(solution)/shard_map/all_to_all | solution.py:37
  86.0 8.7 %convolution_bitcast_fusion = f32[384,2048]{0,1:T(8,128)} fusion(bf16[2048,2048]{1,0:T(8,128)(2,1)} %fusion, bf16[384,2048]{1,0:T(8,128)(2,1)S(1)} %bitcast.73), kind=kOutput, calls=%fused_computation.13 | convolution fusion | flops 3221225472 | bytes 13107200 | tf_op jit(solution)/shard_map/dot_general | solution.py:41
  94.7 3.6 %copy.23 = f32[384,2048]{1,0:T(8,128)} copy(f32[384,2048]{0,1:T(8,128)} %convolution_bitcast_fusion) | data formatting | bytes 6291456
  98.3 0.0 reduce-scatter.4.cloned.1.call-update
  98.3 0.0 all-gather.4.cloned.1.call-start
  98.4 0.0 copy-done.4
  98.4 0.2 broadcast_in_dim.2
  98.6 0.3 reshape.53
  98.8 58.1 %reduce-scatter.4.cloned.1.call-done = f32[96,2048]{1,0:T(8,128)} async-done(((f32[384,2048]{1,0:T(8,128)}), f32[96,2048]{1,0:T(8,128)}) %reduce-scatter.4.cloned.1.call-update) | async-done | bytes 786448
  156.9 1.4 copy.24
  158.3 0.2 slice.96
  158.5 2.4 collective-permute-start
  160.9 0.6 fusion.26
  161.5 1.3 copy.19
  162.8 2.0 copy.17
  164.8 0.0 collective-permute-done
  164.8 1.3 maximum_convert_fusion
  166.1 4.9 %convert_multiply_fusion = f32[96,2048]{0,1:T(8,128)S(1)} fusion(f32[102,2048]{0,1:T(8,128)S(1)} %maximum_convert_fusion, bf16[1,1,96,2048]{2,3,1,0:T(8,128)(2,1)S(1)} %copy.19, bf16[1,1,96,2048]{2,3,1,0:T(8,128)(2,1)} %copy.17, f32[2048]{0:T(1024)S(1)} %bitcast.79, f32[2048]{0:T(1024)} %bitcast.81, f32[2048]{0:T(1024)} %bitcast.83, f32[2048]{0:T(1024)} %bitcast.85, ...), kind=kLoop, calls=%fused_computation.14 | loop fusion | flops 3735552 | bytes 7135232 | tf_op jit(solution)/shard_map/mul | solution.py:54
  171.1 0.3 copy.20
  171.4 1.5 collective-permute-start.1
  172.9 1.7 collective-permute-done.1
  174.5 1.3 copy.21
  175.9 9.6 %fusion.6 = bf16[96,2048]{0,1:T(8,128)(2,1)S(1)} fusion(f32[6,2048]{0,1:T(8,128)} %copy.21, f32[96,2048]{0,1:T(8,128)S(1)} %convert_multiply_fusion, f32[2048]{0:T(1024)S(1)} %bitcast.80, f32[2048]{0:T(1024)} %bitcast.82, f32[2048]{0:T(1024)} %bitcast.84, f32[2048]{0:T(1024)} %bitcast.86, f32[2048]{0:T(1024)} %bitcast.88, f32[2048]{0:T(1024)} %bitcast.90, ...), kind=kLoop, calls=%fused_computation.21 | loop fusion | flops 3932160 | bytes 1286144 | tf_op jit(solution)/shard_map/convert_element_type | solution.py:60
  185.5 0.0 copy-start.1
  185.5 0.0 copy-start.3
  185.5 1.0 copy.22
  186.5 0.0 all-gather.4.cloned.1.call-update
  186.5 0.0 all-reduce.3.cloned.1.call-start
  186.6 37.5 %all-gather.4.cloned.1.call-done = bf16[384,2048]{1,0:T(8,128)(2,1)} async-done(((bf16[96,2048]{1,0:T(8,128)(2,1)}), bf16[384,2048]{1,0:T(8,128)(2,1)}) %all-gather.4.cloned.1.call-update) | async-done | bytes 1572880 | tf_op jit(solution)/shard_map/all_gather | solution.py:61
  224.0 15.7 %divide_reduce_fusion = (f32[16,2048]{1,0:T(8,128)S(1)}, f32[16,2048]{1,0:T(8,128)S(1)}, f32[16,2048]{1,0:T(8,128)S(1)}, f32[16,2048]{1,0:T(8,128)S(1)}) fusion(f32[16,2048]{1,0:T(8,128)S(1)} %get-tuple-element.9, f32[16,2048]{1,0:T(8,128)S(1)} %get-tuple-element.12, bf16[2048,2048]{1,0:T(8,128)(2,1)} %param.8, f32[16,2048]{1,0:T(8,128)} %get-tuple-element.8, ...), kind=kOutput, calls=%fused_computation.12 | convolution fusion | flops 3288203264 | bytes 12451840 | tf_op jit(solution)/shard_map/dot_general | solution.py:62
  239.8 0.8 fusion.25
  240.6 0.0 all-reduce.3.cloned.1.call-update
  240.6 17.3 %all-reduce.3.cloned.1.call-done = (f32[16,2048]{1,0:T(8,128)}, f32[16,2048]{1,0:T(8,128)}) async-done(((f32[16,2048]{1,0:T(8,128)}, f32[16,2048]{1,0:T(8,128)}), (f32[16,2048]{1,0:T(8,128)}, f32[16,2048]{1,0:T(8,128)})) %all-reduce.3.cloned.1.call-update) | async-done | bytes 262160 | tf_op jit(solution)/shard_map/psum | solution.py:71
  258.0 1.6 copy.27
  259.5 1.6 copy.28
  (4 shorter events, 0.0 us)
Async XLA Ops:
  7.2 32.3 %all-gather.6.cloned.1.call-start = ((), (), s32[]{:S(2)}) async-start(), calls=%async_computation.3 | async-start | bytes 2359296 | tf_op jit(solution)/shard_map/all_gather | solution.py:35
  7.9 46.8 %copy-start = (f32[16,2048]{1,0:T(8,128)S(1)}, f32[16,2048]{1,0:T(8,128)}, u32[]{:S(2)}) copy-start(f32[16,2048]{1,0:T(8,128)} %param.10) | copy-start | bytes 393220
  7.9 46.8 %copy-start.2 = (f32[16,2048]{1,0:T(8,128)S(1)}, f32[16,2048]{1,0:T(8,128)}, u32[]{:S(2)}) copy-start(f32[16,2048]{1,0:T(8,128)} %param.9) | copy-start | bytes 393220
  44.4 41.6 %all-to-all-start = ((bf16[4,96,2048]{2,1,0:T(8,128)(2,1)}), bf16[4,96,2048]{2,1,0:T(8,128)(2,1)S(1)}, u32[]{:S(2)}, u32[]{:S(2)}) async-start(bf16[4,96,2048]{2,1,0:T(8,128)(2,1)} %copy.18), calls=%async_computation | async-start | bytes 3145728 | tf_op jit(solution)/shard_map/all_to_all | solution.py:37
  49.0 107.9 %reduce-scatter.4.cloned.1.call-start = ((), (), s32[]{:S(2)}) async-start(), calls=%async_computation.4 | async-start | bytes 3932160
  94.7 3.7 %copy-start.4 = (f32[128,7]{0,1:T(8,128)S(1)}, f32[128,7]{0,1:T(8,128)}, u32[]{:S(2)}) copy-start(f32[128,7]{0,1:T(8,128)} %param.11) | copy-start | bytes 10756
  98.3 125.7 %all-gather.4.cloned.1.call-start = ((), (), s32[]{:S(2)}) async-start(), calls=%async_computation.2 | async-start | bytes 1966080 | tf_op jit(solution)/shard_map/all_gather | solution.py:61
  158.5 6.3 %collective-permute-start = (bf16[6,2048]{0,1:T(8,128)(2,1)S(1)}, bf16[6,2048]{0,1:T(8,128)(2,1)}, u32[]{:S(2)}, u32[]{:S(2)}) collective-permute-start(bf16[6,2048]{0,1:T(8,128)(2,1)S(1)} %slice.96), channel_id=1, source_target_pairs={{0,1},{2,3},{4,5},{6,7},{8,9},{10,11},{12,13},{14,15},{16,17},{18,... | collective-permute-start | bytes 73736 | tf_op jit(solution)/shard_map/ppermute | solution.py:13
  171.4 3.1 %collective-permute-start.1 = (f32[6,2048]{1,0:T(8,128)S(1)}, f32[6,2048]{1,0:T(8,128)S(1)}, u32[]{:S(2)}, u32[]{:S(2)}) collective-permute-start(f32[6,2048]{1,0:T(8,128)S(1)} %copy.20), channel_id=1, source_target_pairs={{1,0},{3,2},{5,4},{7,6},{9,8},{11,10},{13,12},{15,14},{17,16},{19,... | collective-permute-start | bytes 147464 | tf_op jit(solution)/shard_map/ppermute | solution.py:13
  185.5 54.3 %copy-start.1 = (f32[16,2048]{1,0:T(8,128)S(1)}, f32[16,2048]{1,0:T(8,128)}, u32[]{:S(2)}) copy-start(f32[16,2048]{1,0:T(8,128)} %param.10) | copy-start | bytes 393220
  185.5 54.3 %copy-start.3 = (f32[16,2048]{1,0:T(8,128)S(1)}, f32[16,2048]{1,0:T(8,128)}, u32[]{:S(2)}) copy-start(f32[16,2048]{1,0:T(8,128)} %param.9) | copy-start | bytes 393220
  186.5 71.5 %all-reduce.3.cloned.1.call-start = ((), (), s32[]{:S(2)}) async-start(), calls=%async_computation.5 | async-start | bytes 524288 | tf_op jit(solution)/shard_map/psum | solution.py:71
Sparse Core Ops, SparseCore 0:
  9.5 29.8 all-gather.5
  98.5 58.3 reduce-scatter.3
  186.6 37.3 all-gather.3
  240.8 17.1 all-reduce.2
where the time goes:
time: 268 us
  waiting for transfers between devices  169 us (63%)
  other arithmetic  31.9 us (12%)
  matrix products  24.4 us (9%)
  local copies, waits for them, and re-layouts  20.3 us (8%)
  between operations  13.9 us (5%)
  starting transfers between devices  8.55 us (3%)
    unnamed x5, waiting for transfers between devices  58.8 us
    all_gather x1, waiting for transfers between devices, on_device(): d_all = lax.all_gather(d_proj, 'fsdp', axis=0, tiled=True)  37.5 us
    all_gather x1, waiting for transfers between devices, on_device(): features = lax.all_gather(local_rows, 'seq', axis=1, tiled=True)  31.6 us
    all_to_all x1, waiting for transfers between devices, on_device(): mine = lax.all_to_all(pieces, 'fsdp', 0, 0)  21.7 us
    psum x1, waiting for transfers between devices, on_device(): grad_upper, grad_lower = lax.psum((grad_up, grad_low), 'ctx')  17.3 us
    dot_general x1, matrix products, on_device(): lax.dot_general(inputs, d_all, (((0,), (0,)), ((), ())), preferred_elemen...  15.7 us
    unnamed x16, local copies, waits for them, and re-layouts  11.4 us
    convert_element_type x1, other arithmetic, on_device(): d_proj = d_proj.astype(jnp.bfloat16)  9.62 us
  transfers between devices with their start and end apart: 7, of which 6 were waited for; matrix products, arithmetic and copies ran while one was open for 7% of the time, Pallas kernels for 0%

commit v1 on v0

--- a/solution.py
+++ b/solution.py
@@ -5,6 +5,17 @@
 
 FILT = 7
 CGROUP = 16
+
+
+def ring_gather(array, axis, dim):
+    ways = lax.axis_size(axis)
+    pieces = [array]
+    for far in range(1, ways):
+        pieces.append(
+            lax.ppermute(pieces[far - 1], axis, [(d, (d - 1) % ways) for d in range(ways)])
+        )
+    line = jnp.concatenate(pieces, axis=dim)
+    return jnp.roll(line, lax.axis_index(axis) * array.shape[dim], axis=dim)
 
 
 def from_behind(value, axis, by):
@@ -58,7 +69,7 @@
     for tap in range(FILT):
         d_proj = d_proj + taps[tap] * padded_back[tap : tap + length]
     d_proj = d_proj.astype(jnp.bfloat16)
-    d_all = lax.all_gather(d_proj, "fsdp", axis=0, tiled=True)
+    d_all = ring_gather(d_proj, "fsdp", 0)
     d_clipped = lax.dot_general(
         inputs, d_all, (((0,), (0,)), ((), ())), preferred_element_type=jnp.float32
     )

time: 268 us -> 275 us (1.026)
  starting transfers between devices: 8.55 us -> 18.8 us
  other arithmetic: 31.9 us -> 25.9 us
    all_gather x1 -> x0, waiting for transfers between devices: 37.5 us -> none  [on_device(): d_all = lax.all_gather(d_proj, 'fsdp', axis=0, tiled=True)]
    ppermute x0 -> x3, waiting for transfers between devices: none -> 31.9 us  [ring_gather(): lax.ppermute(pieces[far - 1], axis, [(d, (d - 1) % ways) for d in range(w...]
    ppermute x0 -> x3, starting transfers between devices: none -> 11 us  [ring_gather(): lax.ppermute(pieces[far - 1], axis, [(d, (d - 1) % ways) for d in range(w...]
    concatenate x0 -> x1, local copies, waits for them, and re-layouts: none -> 5.74 us  [ring_gather(): return jnp.roll(line, lax.axis_index(axis) * array.shape[dim], axis=dim)]
    convert_element_type x1, other arithmetic: 9.62 us -> 5.69 us  [on_device(): d_proj = d_proj.astype(jnp.bfloat16)]
    psum x1, waiting for transfers between devices: 17.3 us -> 20.5 us  [on_device(): grad_upper, grad_lower = lax.psum((grad_up, grad_low), 'ctx')]
    unnamed x16 -> x28, local copies, waits for them, and re-layouts: 11.4 us -> 10.4 us
    unnamed x5 -> x4, waiting for transfers between devices: 58.8 us -> 58.8 us
  transfers between devices with their start and end apart: 7 -> 9, of which waited for: 6 -> 9; matrix products, arithmetic and copies ran while one was open for 7% -> 6% of each run, Pallas kernels for 0% -> 0%
where the time goes in v1:
time: 275 us; the launch traced here: 274 us
  waiting for transfers between devices  167 us (61%)
  matrix products  26 us (9%)
  other arithmetic  25.9 us (9%)
  local copies, waits for them, and re-layouts  22.4 us (8%)
  starting transfers between devices  18.8 us (7%)
  between operations  14 us (5%)
    unnamed x4, waiting for transfers between devices  58.8 us
    ppermute x3, waiting for transfers between devices, ring_gather(): lax.ppermute(pieces[far - 1], axis, [(d, (d - 1) % ways) for d in range(w...  31.9 us
    all_gather x1, waiting for transfers between devices, on_device(): features = lax.all_gather(local_rows, 'seq', axis=1, tiled=True)  31.6 us
    all_to_all x1, waiting for transfers between devices, on_device(): mine = lax.all_to_all(pieces, 'fsdp', 0, 0)  21.7 us
    psum x1, waiting for transfers between devices, on_device(): grad_upper, grad_lower = lax.psum((grad_up, grad_low), 'ctx')  20.5 us
    dot_general x1, matrix products, on_device(): lax.dot_general(inputs, d_all, (((0,), (0,)), ((), ())), preferred_elemen...  16.8 us
    ppermute x3, starting transfers between devices, ring_gather(): lax.ppermute(pieces[far - 1], axis, [(d, (d - 1) % ways) for d in range(w...  11 us
    unnamed x28, local copies, waits for them, and re-layouts  10.4 us
  transfers between devices with their start and end apart: 9, of which 9 were waited for; matrix products, arithmetic and copies ran while one was open for 6% of the time, Pallas kernels for 0%

profile of v1, /device:TPU:0, one launch (start us, length us, event | category | flops | bytes accessed | tf_op | source)
XLA Modules:
  0.0 274.1 jit_solution(8011540311231080393)
XLA Ops:
  7.2 0.0 all-gather.3.cloned.1.call-start
  7.2 0.7 all-gather.3.cloned.1.call-update
  7.9 0.0 copy-start.4
  7.9 0.0 copy-start.6
  7.9 31.6 %all-gather.3.cloned.1.call-done = bf16[1,1,96,8192]{3,2,1,0:T(8,128)(2,1)} async-done(((bf16[1,1,96,4096]{3,2,1,0:T(8,128)(2,1)}), bf16[1,1,96,8192]{3,2,1,0:T(8,128)(2,1)}) %all-gather.3.cloned.1.call-update) | async-done | bytes 1572880 | tf_op jit(solution)/shard_map/all_gather | solution.py:46
  39.5 2.9 %reshape.56 = bf16[96,4,2048]{2,1,0:T(4,128)(2,1)S(1)} reshape(bf16[1,1,96,8192]{3,2,1,0:T(8,128)(2,1)} %all-gather.3.cloned.1.call-done) | data formatting | bytes 3145728 | tf_op jit(solution)/shard_map/reshape | solution.py:47
  42.4 2.1 copy.18
  44.4 4.6 %all-to-all-start = ((bf16[4,96,2048]{2,1,0:T(8,128)(2,1)}), bf16[4,96,2048]{2,1,0:T(8,128)(2,1)S(1)}, u32[]{:S(2)}, u32[]{:S(2)}) async-start(bf16[4,96,2048]{2,1,0:T(8,128)(2,1)} %copy.18), calls=%async_computation | async-start | bytes 3145728 | tf_op jit(solution)/shard_map/all_to_all | solution.py:48
  49.0 5.7 %abs_reduce_fusion = f32[16,2048]{1,0:T(8,128)S(1)} fusion(bf16[2048,2048]{1,0:T(8,128)(2,1)} %param.8), kind=kLoop, calls=%fused_computation.11 | loop fusion | flops 12550144 | bytes 8519680 | tf_op jit(solution)/shard_map/reduce_max | solution.py:31
  54.7 0.8 multiply_divide_fusion
  55.5 8.8 %fusion = bf16[2048,2048]{1,0:T(8,128)(2,1)} fusion(bf16[2048,2048]{1,0:T(8,128)(2,1)} %param.8, f32[16,2048]{1,0:T(8,128)S(1)} %get-tuple-element.9, f32[16,2048]{1,0:T(8,128)S(1)} %get-tuple-element.12), kind=kLoop, calls=%fused_computation.4 | loop fusion | flops 25165824 | bytes 17039360 | tf_op jit(solution)/shard_map/convert_element_type | solution.py:51
  64.3 21.7 %all-to-all-done = bf16[4,96,2048]{2,1,0:T(8,128)(2,1)S(1)} async-done(((bf16[4,96,2048]{2,1,0:T(8,128)(2,1)}), bf16[4,96,2048]{2,1,0:T(8,128)(2,1)S(1)}, u32[]{:S(2)}, u32[]{:S(2)}) %all-to-all-start) | async-done | bytes 1572896 | tf_op jit(solution)/shard_map/all_to_all | solution.py:48
  86.0 9.3 %convolution_bitcast_fusion = f32[384,2048]{0,1:T(8,128)} fusion(bf16[2048,2048]{1,0:T(8,128)(2,1)} %fusion, bf16[384,2048]{1,0:T(8,128)(2,1)S(1)} %bitcast.72), kind=kOutput, calls=%fused_computation.13 | convolution fusion | flops 3221225472 | bytes 13107200 | tf_op jit(solution)/shard_map/dot_general | solution.py:52
  95.3 3.7 %copy.22 = f32[384,2048]{1,0:T(8,128)} copy(f32[384,2048]{0,1:T(8,128)} %convolution_bitcast_fusion) | data formatting | bytes 6291456
  98.9 0.0 reduce-scatter.4.cloned.1.call-update
  98.9 0.0 all-reduce.3.cloned.1.call-start
  99.0 0.2 broadcast_in_dim.2
  99.2 0.3 reshape.53
  99.4 58.1 %reduce-scatter.4.cloned.1.call-done = f32[96,2048]{1,0:T(8,128)} async-done(((f32[384,2048]{1,0:T(8,128)}), f32[96,2048]{1,0:T(8,128)}) %reduce-scatter.4.cloned.1.call-update) | async-done | bytes 786448
  157.5 1.4 copy.23
  158.9 0.2 slice.96
  159.1 1.6 collective-permute-start
  160.8 0.3 copy.19
  161.1 0.3 copy.17
  161.4 0.9 collective-permute-done
  162.2 0.3 maximum_convert_fusion
  162.5 3.9 %convert_multiply_fusion = f32[96,2048]{0,1:T(8,128)S(1)} fusion(f32[102,2048]{0,1:T(8,128)S(1)} %maximum_convert_fusion, bf16[1,1,96,2048]{2,3,1,0:T(8,128)(2,1)S(1)} %copy.19, bf16[1,1,96,2048]{2,3,1,0:T(8,128)(2,1)S(1)} %copy.17, f32[2048]{0:T(1024)S(1)} %bitcast.78, f32[2048]{0:T(1024)S(1)} %bitcast.80, f32[2048]{0:T(1024)S(1)} %bitcast.82, ...), kind=kLoop, calls=%fused_computation.16 | loop fusion | flops 3735552 | bytes 7135232 | tf_op jit(solution)/shard_map/mul | solution.py:65
  166.4 0.3 copy.20
  166.7 1.5 collective-permute-start.1
  168.2 1.7 collective-permute-done.1
  169.8 0.4 copy.21
  170.2 5.7 %fusion.8 = bf16[96,2048]{0,1:T(8,128)(2,1)S(1)} fusion(f32[6,2048]{0,1:T(8,128)S(1)} %copy.21, f32[96,2048]{0,1:T(8,128)S(1)} %convert_multiply_fusion, f32[2048]{0:T(1024)S(1)} %bitcast.79, f32[2048]{0:T(1024)S(1)} %bitcast.81, f32[2048]{0:T(1024)S(1)} %bitcast.83, f32[2048]{0:T(1024)S(1)} %bitcast.85, f32[2048]{0:T(1024)S(1)} %bitcast.87, ...), kind=kLoop, calls=%fused_computation.23 | loop fusion | flops 3932160 | bytes 1286144 | tf_op jit(solution)/shard_map/convert_element_type | solution.py:71
  175.9 0.8 copy-done.1
  176.7 2.5 collective-permute-start.2
  179.2 11.5 %collective-permute-done.2 = bf16[96,2048]{0,1:T(8,128)(2,1)S(1)} collective-permute-done((bf16[96,2048]{0,1:T(8,128)(2,1)S(1)}, bf16[96,2048]{0,1:T(8,128)(2,1)S(1)}, u32[]{:S(2)}, u32[]{:S(2)}) %collective-permute-start.2) | collective-permute-done | bytes 393248 | tf_op jit(solution)/shard_map/ppermute | solution.py:15
  190.7 0.8 copy-done.2
  191.5 4.3 %collective-permute-start.3 = (bf16[96,2048]{0,1:T(8,128)(2,1)S(1)}, bf16[96,2048]{0,1:T(8,128)(2,1)S(1)}, u32[]{:S(2)}, u32[]{:S(2)}) collective-permute-start(bf16[96,2048]{0,1:T(8,128)(2,1)S(1)} %collective-permute-done.2), channel_id=1, source_target_pairs={{0,12},{4,0},{8,4},{12,8},{1,13},{5,1},{9,5},{13,9},{2,14},{6,2},{... | collective-permute-start | bytes 1179656 | tf_op jit(solution)/shard_map/ppermute | solution.py:15
  195.8 10.7 %collective-permute-done.3 = bf16[96,2048]{0,1:T(8,128)(2,1)S(1)} collective-permute-done((bf16[96,2048]{0,1:T(8,128)(2,1)S(1)}, bf16[96,2048]{0,1:T(8,128)(2,1)S(1)}, u32[]{:S(2)}, u32[]{:S(2)}) %collective-permute-start.3) | collective-permute-done | bytes 393248 | tf_op jit(solution)/shard_map/ppermute | solution.py:15
  206.4 4.3 %collective-permute-start.4 = (bf16[96,2048]{0,1:T(8,128)(2,1)S(1)}, bf16[96,2048]{0,1:T(8,128)(2,1)}, u32[]{:S(2)}, u32[]{:S(2)}) collective-permute-start(bf16[96,2048]{0,1:T(8,128)(2,1)S(1)} %collective-permute-done.3), channel_id=1, source_target_pairs={{0,12},{4,0},{8,4},{12,8},{1,13},{5,1},{9,5},{13,9},{2,14},{6,2},{... | collective-permute-start | bytes 1179656 | tf_op jit(solution)/shard_map/ppermute | solution.py:15
  210.7 9.7 %collective-permute-done.4 = bf16[96,2048]{0,1:T(8,128)(2,1)} collective-permute-done((bf16[96,2048]{0,1:T(8,128)(2,1)S(1)}, bf16[96,2048]{0,1:T(8,128)(2,1)}, u32[]{:S(2)}, u32[]{:S(2)}) %collective-permute-start.4) | collective-permute-done | bytes 393248 | tf_op jit(solution)/shard_map/ppermute | solution.py:15
  220.5 5.7 %concatenate.14 = bf16[768,2048]{0,1:T(8,128)(2,1)S(1)} concatenate(bf16[96,2048]{0,1:T(8,128)(2,1)} %copy-done.1, bf16[96,2048]{0,1:T(8,128)(2,1)} %copy-done.2, bf16[96,2048]{0,1:T(8,128)(2,1)} %copy-done.3, bf16[96,2048]{0,1:T(8,128)(2,1)} %collective-permute-done.4, bf16[96,2048]{0,1:T(8,128)(2,1)} %copy-done.1, bf16[96,2048]{0,1:T(8,128)(2,1)} %copy-done.2, ...), dimensions={0} | concatenate | bytes 6291456 | tf_op jit(solution)/shard_map/jit(_roll_dynamic)/concatenate | solution.py:18
  226.2 0.0 copy-start.5
  226.3 16.8 %divide_reduce_fusion = (f32[16,2048]{1,0:T(8,128)S(1)}, f32[16,2048]{1,0:T(8,128)S(1)}, f32[16,2048]{1,0:T(8,128)S(1)}, f32[16,2048]{1,0:T(8,128)S(1)}) fusion(f32[16,2048]{1,0:T(8,128)S(1)} %get-tuple-element.9, f32[16,2048]{1,0:T(8,128)S(1)} %get-tuple-element.12, bf16[2048,2048]{1,0:T(8,128)(2,1)} %param.8, f32[16,2048]{1,0:T(8,128)} %get-tuple-element.8, ...), kind=kOutput, calls=%fused_computation.12 | convolution fusion | flops 3288203264 | bytes 12451844 | tf_op jit(solution)/shard_map/dot_general | solution.py:73
  243.1 0.8 fusion.27
  243.9 0.0 all-reduce.3.cloned.1.call-update
  243.9 20.5 %all-reduce.3.cloned.1.call-done = (f32[16,2048]{1,0:T(8,128)}, f32[16,2048]{1,0:T(8,128)}) async-done(((f32[16,2048]{1,0:T(8,128)}, f32[16,2048]{1,0:T(8,128)}), (f32[16,2048]{1,0:T(8,128)}, f32[16,2048]{1,0:T(8,128)})) %all-reduce.3.cloned.1.call-update) | async-done | bytes 262160 | tf_op jit(solution)/shard_map/psum | solution.py:82
  264.4 1.6 copy.26
  266.0 1.6 copy.27
  (19 shorter events, 0.1 us)
Async XLA Ops:
  7.2 32.3 %all-gather.3.cloned.1.call-start = ((), (), s32[]{:S(2)}) async-start(), calls=%async_computation.2 | async-start | bytes 2359296 | tf_op jit(solution)/shard_map/all_gather | solution.py:46
  7.9 46.8 %copy-start.4 = (f32[16,2048]{1,0:T(8,128)S(1)}, f32[16,2048]{1,0:T(8,128)}, u32[]{:S(2)}) copy-start(f32[16,2048]{1,0:T(8,128)} %param.10) | copy-start | bytes 393220
  7.9 46.8 %copy-start.6 = (f32[16,2048]{1,0:T(8,128)S(1)}, f32[16,2048]{1,0:T(8,128)}, u32[]{:S(2)}) copy-start(f32[16,2048]{1,0:T(8,128)} %param.9) | copy-start | bytes 393220
  44.4 41.6 %all-to-all-start = ((bf16[4,96,2048]{2,1,0:T(8,128)(2,1)}), bf16[4,96,2048]{2,1,0:T(8,128)(2,1)S(1)}, u32[]{:S(2)}, u32[]{:S(2)}) async-start(bf16[4,96,2048]{2,1,0:T(8,128)(2,1)} %copy.18), calls=%async_computation | async-start | bytes 3145728 | tf_op jit(solution)/shard_map/all_to_all | solution.py:48
  49.0 108.5 %reduce-scatter.4.cloned.1.call-start = ((), (), s32[]{:S(2)}) async-start(), calls=%async_computation.3 | async-start | bytes 3932160
  86.0 9.3 %copy-start = (bf16[4,96,2048]{2,1,0:T(8,128)(2,1)}, bf16[4,96,2048]{2,1,0:T(8,128)(2,1)S(1)}, u32[]{:S(2)}) copy-start(bf16[4,96,2048]{2,1,0:T(8,128)(2,1)S(1)} %all-to-all-done) | copy-start | bytes 4718596
  95.2 3.8 %copy-start.10 = (f32[128,7]{0,1:T(8,128)S(1)}, f32[128,7]{0,1:T(8,128)}, u32[]{:S(2)}) copy-start(f32[128,7]{0,1:T(8,128)} %param.11) | copy-start | bytes 10756
  95.2 65.5 %copy-start.8 = (bf16[1,1,96,2048]{3,2,1,0:T(8,128)(2,1)S(1)}, bf16[1,1,96,2048]{3,2,1,0:T(8,128)(2,1)}, u32[]{:S(2)}) copy-start(bf16[1,1,96,2048]{3,2,1,0:T(8,128)(2,1)} %param.13) | copy-start | bytes 1179652
  95.3 65.8 %copy-start.9 = (bf16[1,1,96,2048]{3,2,1,0:T(8,128)(2,1)S(1)}, bf16[1,1,96,2048]{3,2,1,0:T(8,128)(2,1)}, u32[]{:S(2)}) copy-start(bf16[1,1,96,2048]{3,2,1,0:T(8,128)(2,1)} %param.12) | copy-start | bytes 1179652
  98.9 165.5 %all-reduce.3.cloned.1.call-start = ((), (), s32[]{:S(2)}) async-start(), calls=%async_computation.4 | async-start | bytes 524288 | tf_op jit(solution)/shard_map/psum | solution.py:82
  159.1 3.1 %collective-permute-start = (bf16[6,2048]{0,1:T(8,128)(2,1)S(1)}, bf16[6,2048]{0,1:T(8,128)(2,1)S(1)}, u32[]{:S(2)}, u32[]{:S(2)}) collective-permute-start(bf16[6,2048]{0,1:T(8,128)(2,1)S(1)} %slice.96), channel_id=1, source_target_pairs={{0,1},{2,3},{4,5},{6,7},{8,9},{10,11},{12,13},{14,15},{16,17},{18,... | collective-permute-start | bytes 73736 | tf_op jit(solution)/shard_map/ppermute | solution.py:24
  166.7 3.1 %collective-permute-start.1 = (f32[6,2048]{1,0:T(8,128)S(1)}, f32[6,2048]{1,0:T(8,128)S(1)}, u32[]{:S(2)}, u32[]{:S(2)}) collective-permute-start(f32[6,2048]{1,0:T(8,128)S(1)} %copy.20), channel_id=1, source_target_pairs={{1,0},{3,2},{5,4},{7,6},{9,8},{11,10},{13,12},{15,14},{17,16},{19,... | collective-permute-start | bytes 147464 | tf_op jit(solution)/shard_map/ppermute | solution.py:24
  175.9 0.8 copy-start.1
  176.7 14.0 %collective-permute-start.2 = (bf16[96,2048]{0,1:T(8,128)(2,1)S(1)}, bf16[96,2048]{0,1:T(8,128)(2,1)S(1)}, u32[]{:S(2)}, u32[]{:S(2)}) collective-permute-start(bf16[96,2048]{0,1:T(8,128)(2,1)S(1)} %fusion.8), channel_id=1, source_target_pairs={{0,12},{4,0},{8,4},{12,8},{1,13},{5,1},{9,5},{13,9},{2,14},{6,2},{... | collective-permute-start | bytes 1179656 | tf_op jit(solution)/shard_map/ppermute | solution.py:15
  190.7 0.8 copy-start.2
  191.5 14.9 %collective-permute-start.3 = (bf16[96,2048]{0,1:T(8,128)(2,1)S(1)}, bf16[96,2048]{0,1:T(8,128)(2,1)S(1)}, u32[]{:S(2)}, u32[]{:S(2)}) collective-permute-start(bf16[96,2048]{0,1:T(8,128)(2,1)S(1)} %collective-permute-done.2), channel_id=1, source_target_pairs={{0,12},{4,0},{8,4},{12,8},{1,13},{5,1},{9,5},{13,9},{2,14},{6,2},{... | collective-permute-start | bytes 1179656 | tf_op jit(solution)/shard_map/ppermute | solution.py:15
  206.4 4.3 %copy-start.3 = (bf16[96,2048]{0,1:T(8,128)(2,1)}, bf16[96,2048]{0,1:T(8,128)(2,1)S(1)}, u32[]{:S(2)}) copy-start(bf16[96,2048]{0,1:T(8,128)(2,1)S(1)} %collective-permute-done.3) | copy-start | bytes 1179652
  206.4 14.0 %collective-permute-start.4 = (bf16[96,2048]{0,1:T(8,128)(2,1)S(1)}, bf16[96,2048]{0,1:T(8,128)(2,1)}, u32[]{:S(2)}, u32[]{:S(2)}) collective-permute-start(bf16[96,2048]{0,1:T(8,128)(2,1)S(1)} %collective-permute-done.3), channel_id=1, source_target_pairs={{0,12},{4,0},{8,4},{12,8},{1,13},{5,1},{9,5},{13,9},{2,14},{6,2},{... | collective-permute-start | bytes 1179656 | tf_op jit(solution)/shard_map/ppermute | solution.py:15
  226.2 16.8 %copy-start.5 = (f32[16,2048]{1,0:T(8,128)S(1)}, f32[16,2048]{1,0:T(8,128)}, u32[]{:S(2)}) copy-start(f32[16,2048]{1,0:T(8,128)} %param.10) | copy-start | bytes 393220
  226.2 16.8 %copy-start.7 = (f32[16,2048]{1,0:T(8,128)S(1)}, f32[16,2048]{1,0:T(8,128)}, u32[]{:S(2)}) copy-start(f32[16,2048]{1,0:T(8,128)} %param.9) | copy-start | bytes 393220
Sparse Core Ops, SparseCore 0:
  9.5 29.8 all-gather.2
  99.1 58.3 reduce-scatter.3
  244.0 20.3 all-reduce.2
